TPU v7x, 128 devices: a whole 4x4x4 slice. The times are simulated.
128 devices in a mesh: dp: 8 (over x, core), pair: 16 (over z, y).
Axes of the slice: x: 4, y: 4, z: 4, core: 2. Of those that a mesh axis runs over, the one named last changes fastest.
Arguments:
- anchor: bfloat16 [5, 4096, 1024], P(None, ('dp', 'pair')), may hold values from -20 to 20
- partner: bfloat16 [5, 4096, 1024], P(None, ('dp', 'pair')), may hold values from -12 to 12
- counts: int32 [5], replicated, may hold values from 512 to 4096, as said below
- pair_scale: float32 [5], replicated, may hold values from 2 to 8
Outputs:
- loss_value: float32 [], replicated
- grad_anchor: float32 [5, 4096, 1024], P(None, ('dp', 'pair'))
- grad_partner: float32 [5, 4096, 1024], P(None, ('dp', 'pair'))
Inputs may be any that keep to these rules, and one draw needn't show every extreme that they name: The valid samples of pair p are its rows 0 to counts[p] - 1; one pair has all 4096 rows valid.
All inputs are finite; a program needn't handle non-finite values.
Results may differ from a plain program's by a relative error of at most 0.0021.
Values may be sent and summed in bfloat16 or wider, within the bound.
No kernel may reach another device: no remote copies, remote signals or barrier semaphores. Data moves between devices by JAX's collectives and lax.ppermute only.
A program may use at most 128 MiB of HBM per device.

v0:
```python
import math
import jax
import jax.numpy as jnp
from jax import lax
from jax.sharding import PartitionSpec as P

NEG = -1e30


def merge_pair(mine, other):
    highest = jnp.maximum(mine[0], other[0])
    summed = mine[1] * jnp.exp(mine[0] - highest) + other[1] * jnp.exp(other[0] - highest)
    return jnp.concatenate([highest[None], summed[None], mine[2:] + other[2:]], axis=0)


def butterfly_merge(stats, axis, size):
    own = lax.axis_index(axis)
    bit = 1
    while bit < size:
        other = lax.ppermute(stats, axis, [(i, i ^ bit) for i in range(size)])
        lower = own & bit == 0
        stats = merge_pair(jnp.where(lower, stats, other), jnp.where(lower, other, stats))
        bit *= 2
    return stats


def group_merge(stats, axis, stride, group):
    own = lax.axis_index(axis)
    digit = own // stride % group
    size = lax.axis_size(axis)
    received = [stats]
    for shift in range(1, group):
        perm = [
            (i, i + ((i // stride + shift) % group - i // stride % group) * stride)
            for i in range(size)
        ]
        received.append(lax.ppermute(stats, axis, perm))
    stacked = jnp.stack(received)
    ordered = jnp.take(stacked, (digit - jnp.arange(group)) % group, axis=0)
    merged = ordered[0]
    for member in range(1, group):
        merged = merge_pair(merged, ordered[member])
    return merged


def butterfly_sum(values, axis, size):
    own = lax.axis_index(axis)
    bit = 1
    while bit < size:
        other = lax.ppermute(values, axis, [(i, i ^ bit) for i in range(size)])
        lower = own & bit == 0
        values = jnp.where(lower, values, other) + jnp.where(lower, other, values)
        bit *= 2
    return values


def ring_position(offset, size):
    return (offset + size // 2) % size


def ring_gather(shard, axis, size):
    forward = [(i, (i + 1) % size) for i in range(size)]
    backward = [(i, (i - 1) % size) for i in range(size)]
    parts = [None] * size
    parts[ring_position(0, size)] = shard
    ahead = shard
    behind = shard
    forward_steps = size // 2
    backward_steps = size - 1 - forward_steps
    for step in range(1, forward_steps + 1):
        ahead = lax.ppermute(ahead, axis, forward)
        parts[ring_position(-step, size)] = ahead
        if step <= backward_steps:
            behind = lax.ppermute(behind, axis, backward)
            parts[ring_position(step, size)] = behind
    return parts


def two_stage_reduce_scatter(grad_cols, extra, axis, size, shard_rows):
    pair_count, _, width = grad_cols.shape
    own = lax.axis_index(axis)
    parity = own % 2
    chips = size // 2
    by_chip = grad_cols.reshape(pair_count, chips, 2, shard_rows, width)
    keep = lax.dynamic_index_in_dim(by_chip, parity, axis=2, keepdims=False)
    send = lax.dynamic_index_in_dim(by_chip, 1 - parity, axis=2, keepdims=False)
    body_rows = pair_count * chips * shard_rows
    send = jnp.concatenate([send.reshape(body_rows, width), extra], axis=0)
    got = lax.ppermute(send, axis, [(i, i ^ 1) for i in range(size)])
    summed = keep + got[:body_rows].reshape(pair_count, chips, shard_rows, width)
    carried = extra + got[body_rows:]
    chip = own // 2
    ring = [(i, (i + 2) % size) for i in range(size)]
    chunk_rows = pair_count * shard_rows

    def addend(target):
        block = lax.dynamic_index_in_dim(summed, target % chips, axis=1, keepdims=False)
        return jnp.concatenate([block.reshape(chunk_rows, width), carried], axis=0)

    running = addend(chip - 1)
    for step in range(1, chips):
        running = lax.ppermute(running, axis, ring) + addend(chip - 1 - step)
    return (running[:chunk_rows].reshape(pair_count, shard_rows, width), running[chunk_rows])


def per_device(anchor, partner, counts, pair_scale):
    pair_count, shard_rows, model_width = anchor.shape
    score_scale = 4.0 / math.sqrt(model_width)
    dp_size = lax.axis_size("dp")
    pair_size = lax.axis_size("pair")
    dp_index = lax.axis_index("dp")
    pair_place = lax.axis_index("pair")
    own_first = (dp_index * pair_size + pair_place) * shard_rows
    offsets = jnp.arange(shard_rows, dtype=jnp.int32)
    own_valid = own_first + offsets[None, :] < counts[:, None]
    positive = (
        jnp.sum(anchor.astype(jnp.float32) * partner.astype(jnp.float32), axis=2) * score_scale
    )
    own_positive = jnp.sum(jnp.where(own_valid, positive, 0.0), axis=1)
    row_set = lax.all_gather(anchor, "pair", axis=1, tiled=True)
    col_set = jnp.concatenate(ring_gather(partner, "dp", dp_size), axis=1)
    col_set = jnp.roll(col_set, (dp_index - dp_size // 2) * shard_rows, axis=1)
    row_count = row_set.shape[1]
    col_count = col_set.shape[1]
    row_global = dp_index * row_count + jnp.arange(row_count, dtype=jnp.int32)
    col_first = (jnp.arange(dp_size, dtype=jnp.int32) * pair_size + pair_place) * shard_rows
    col_global = (col_first[:, None] + offsets[None, :]).reshape(-1)
    row_valid = row_global[None, :] < counts[:, None]
    col_valid = col_global[None, :] < counts[:, None]
    inside = row_valid[:, :, None] & col_valid[:, None, :]
    scores = (
        jnp.einsum("prd,pcd->prc", row_set, col_set, preferred_element_type=jnp.float32)
        * score_scale
    )
    masked = jnp.where(inside, scores, NEG)
    row_high = jnp.max(masked, axis=2)
    row_sum = jnp.sum(jnp.where(inside, jnp.exp(masked - row_high[:, :, None]), 0.0), axis=2)
    col_high = jnp.max(masked, axis=1)
    col_sum = jnp.sum(jnp.where(inside, jnp.exp(masked - col_high[:, None, :]), 0.0), axis=1)
    col_stats = jnp.stack([col_high, col_sum])
    col_stats = group_merge(group_merge(col_stats, "dp", 1, 2), "dp", 2, dp_size // 2)
    col_high, col_sum = (col_stats[0], col_stats[1])
    col_lse = jnp.where(col_valid, col_high + jnp.log(jnp.where(col_valid, col_sum, 1.0)), 0.0)
    lanes = jnp.arange(row_count, dtype=jnp.int32)[None, :]
    carried = jnp.where(lanes == 0, own_positive[:, None], 0.0)
    row_stats = jnp.stack([row_high, row_sum, carried])
    row_stats = group_merge(group_merge(row_stats, "pair", 1, 4), "pair", 4, pair_size // 4)
    row_high, row_sum, carried = (row_stats[0], row_stats[1], row_stats[2])
    row_lse = jnp.where(row_valid, row_high + jnp.log(jnp.where(row_valid, row_sum, 1.0)), 0.0)
    row_part = jnp.sum(row_lse, axis=1) - 2.0 * carried[:, 0]
    prob_row = jnp.where(inside, jnp.exp(scores - row_lse[:, :, None]), 0.0)
    prob_col = jnp.where(inside, jnp.exp(scores - col_lse[:, None, :]), 0.0)
    weights = (pair_scale[:, None, None] * 0.5 * (prob_row + prob_col)).astype(jnp.bfloat16)
    weights = lax.optimization_barrier(weights)
    grad_rows = (
        jnp.einsum("prc,pcd->prd", weights, col_set, preferred_element_type=jnp.float32)
        * score_scale
    )
    grad_cols = (
        jnp.einsum("prc,prd->pcd", weights, row_set, preferred_element_type=jnp.float32)
        * score_scale
    )
    anchor_part = lax.psum_scatter(grad_rows, "pair", scatter_dimension=1, tiled=True)
    width_lanes = jnp.arange(model_width, dtype=jnp.int32)[None, :]
    slots = (jnp.arange(pair_count, dtype=jnp.int32) * dp_size + dp_index)[:, None]
    loss_row = jnp.sum(jnp.where(width_lanes == slots, row_part[:, None], 0.0), axis=0)
    extra = jnp.concatenate([loss_row[None], jnp.zeros((7, model_width), jnp.float32)], axis=0)
    partner_part, loss_row = two_stage_reduce_scatter(grad_cols, extra, "dp", dp_size, shard_rows)
    row_parts = loss_row[: pair_count * dp_size].reshape(pair_count, dp_size)
    col_total = butterfly_sum(jnp.sum(col_lse, axis=1), "pair", pair_size)
    totals = col_total + jnp.sum(row_parts, axis=1)
    loss_value = jnp.sum(totals / (2.0 * counts.astype(jnp.float32))) / pair_count
    own_term = (pair_scale * score_scale)[:, None, None]
    keep_rows = own_valid[:, :, None]
    anchor_out = jnp.where(keep_rows, anchor_part - own_term * partner.astype(jnp.float32), 0.0)
    partner_out = jnp.where(keep_rows, partner_part - own_term * anchor.astype(jnp.float32), 0.0)
    return (loss_value, anchor_out, partner_out)


def solution(mesh):
    in_specs = (P(None, ("dp", "pair"), None), P(None, ("dp", "pair"), None), P(), P())
    out_specs = (P(), P(None, ("dp", "pair"), None), P(None, ("dp", "pair"), None))
    return jax.shard_map(
        per_device, mesh=mesh, in_specs=in_specs, out_specs=out_specs, check_vma=False
    )
```

profile of v0, /device:TPU:1, one launch (start us, length us, event | category | flops | bytes accessed | tf_op | source)
XLA Modules:
  0.0 210.4 jit_solution(16853269041058675096)
XLA Ops:
  8.0 2.6 %collective-permute-start = (bf16[5,32,1024]{2,1,0:T(8,128)(2,1)}, bf16[5,32,1024]{2,1,0:T(8,128)(2,1)S(1)}, u32[]{:S(2)}, u32[]{:S(2)}) collective-permute-start(bf16[5,32,1024]{2,1,0:T(8,128)(2,1)} %param.7), channel_id=1, source_target_pairs={{0,16},{16,32},{32,48},{48,64},{64,80},{80,96},{96,112},{112,0},{1... | collective-permute-start | bytes 983048 | tf_op jit(solution)/shard_map/ppermute | solution.py:71
  14.9 2.4 %collective-permute-start.1 = (bf16[5,32,1024]{2,1,0:T(8,128)(2,1)S(1)}, bf16[5,32,1024]{2,1,0:T(8,128)(2,1)S(1)}, u32[]{:S(2)}, u32[]{:S(2)}) collective-permute-start(bf16[5,32,1024]{2,1,0:T(8,128)(2,1)S(1)} %collective-permute-done), channel_id=1, source_target_pairs={{0,16},{16,32},{32,48},{48,64},{64,80},{80,96},{96,112},{112,0},{1... | collective-permute-start | bytes 983048 | tf_op jit(solution)/shard_map/ppermute | solution.py:71
  18.0 3.3 %collective-permute-done.1 = bf16[5,32,1024]{2,1,0:T(8,128)(2,1)S(1)} collective-permute-done((bf16[5,32,1024]{2,1,0:T(8,128)(2,1)S(1)}, bf16[5,32,1024]{2,1,0:T(8,128)(2,1)S(1)}, u32[]{:S(2)}, u32[]{:S(2)}) %collective-permute-start.1) | collective-permute-done | bytes 327712 | tf_op jit(solution)/shard_map/ppermute | solution.py:71
  21.3 2.5 %collective-permute-start.2 = (bf16[5,32,1024]{2,1,0:T(8,128)(2,1)S(1)}, bf16[5,32,1024]{2,1,0:T(8,128)(2,1)S(1)}, u32[]{:S(2)}, u32[]{:S(2)}) collective-permute-start(bf16[5,32,1024]{2,1,0:T(8,128)(2,1)S(1)} %collective-permute-done.1), channel_id=1, source_target_pairs={{0,16},{16,32},{32,48},{48,64},{64,80},{80,96},{96,112},{112,0},{1... | collective-permute-start | bytes 983048 | tf_op jit(solution)/shard_map/ppermute | solution.py:71
  27.8 2.5 %collective-permute-start.3 = (bf16[5,32,1024]{2,1,0:T(8,128)(2,1)S(1)}, bf16[5,32,1024]{2,1,0:T(8,128)(2,1)S(1)}, u32[]{:S(2)}, u32[]{:S(2)}) collective-permute-start(bf16[5,32,1024]{2,1,0:T(8,128)(2,1)S(1)} %collective-permute-done.2), channel_id=1, source_target_pairs={{0,16},{16,32},{32,48},{48,64},{64,80},{80,96},{96,112},{112,0},{1... | collective-permute-start | bytes 983048 | tf_op jit(solution)/shard_map/ppermute | solution.py:71
  47.6 22.4 %all-gather.2.cloned.1.call-done = bf16[5,512,1024]{2,1,0:T(8,128)(2,1)} async-done(((bf16[5,32,1024]{2,1,0:T(8,128)(2,1)}), bf16[5,512,1024]{2,1,0:T(8,128)(2,1)}) %all-gather.2.cloned.1.call-update) | async-done | bytes 5242896 | tf_op jit(solution)/shard_map/all_gather | solution.py:120
  69.9 5.2 %fusion.11 = (f32[5,256]{1,0:T(8,128)S(1)}, f32[5,512]{1,0:T(8,128)S(1)}, f32[5,256,512]{2,1,0:T(8,128)S(1)}) fusion(pred[5,256]{1,0:T(8,128)(4,1)S(1)} %broadcast_compare_fusion.1, pred[5,512]{1,0:T(8,128)(4,1)S(1)} %broadcast_compare_fusion, bf16[5,512,1024]{2,1,0:T(8,128)(2,1)} %all-gather.2.cloned.1.call-done, ...), kind=kOutput, calls=%fused_computation.30 | convolution fusion | flops 1345450240 | bytes 10504964 | tf_op jit(solution)/shard_map/prd,pcd->prc/dot_general | solution.py:132
  80.8 2.5 %collective-permute-start.10 = (f32[2,5,256]{2,1,0:T(8,128)S(1)}, f32[2,5,256]{2,1,0:T(8,128)S(1)}, u32[]{:S(2)}, u32[]{:S(2)}) collective-permute-start(f32[2,5,256]{2,1,0:T(8,128)S(1)} %get-tuple-element.34), channel_id=1, source_target_pairs={{0,96},{16,112},{32,0},{48,16},{64,32},{80,48},{96,64},{112,80},{1... | collective-permute-start | bytes 30728 | tf_op jit(solution)/shard_map/ppermute | solution.py:37
  84.5 2.5 %collective-permute-start.17 = (f32[3,5,512]{2,0,1:T(4,128)S(1)}, f32[3,5,512]{2,0,1:T(4,128)S(1)}, u32[]{:S(2)}, u32[]{:S(2)}) collective-permute-start(f32[3,5,512]{2,0,1:T(4,128)S(1)} %get-tuple-element.32), channel_id=1, source_target_pairs={{0,3},{1,0},{2,1},{3,2},{4,7},{5,4},{6,5},{7,6},{8,11},{9,8},{10,9... | collective-permute-start | bytes 92168 | tf_op jit(solution)/shard_map/ppermute | solution.py:37
  88.8 2.6 %collective-permute-done.16 = f32[3,5,512]{2,0,1:T(4,128)S(1)} collective-permute-done((f32[3,5,512]{2,0,1:T(4,128)S(1)}, f32[3,5,512]{2,0,1:T(4,128)S(1)}, u32[]{:S(2)}, u32[]{:S(2)}) %collective-permute-start.16) | collective-permute-done | bytes 30752 | tf_op jit(solution)/shard_map/ppermute | solution.py:37
  95.8 2.5 %collective-permute-done.19 = f32[3,5,512]{2,0,1:T(4,128)S(1)} collective-permute-done((f32[3,5,512]{2,0,1:T(4,128)S(1)}, f32[3,5,512]{2,0,1:T(4,128)S(1)}, u32[]{:S(2)}, u32[]{:S(2)}) %collective-permute-start.19) | collective-permute-done | bytes 30752 | tf_op jit(solution)/shard_map/ppermute | solution.py:37
  99.8 2.7 %fusion.4 = bf16[5,512,256]{1,2,0:T(8,128)(2,1)S(1)} fusion(f32[5,256,512]{2,1,0:T(8,128)} %copy-done.2, f32[5,256]{1,0:T(8,128)S(1)} %get-tuple-element.9, f32[5,512]{1,0:T(8,128)S(1)} %get-tuple-element.13, f32[5]{0:T(128)S(1)} %get-tuple-element.40, pred[5,256]{1,0:T(8,128)(4,1)S(1)} %broadcast_compare_fusion.1, pred[5,512]{1,0:T(8,128)(4,1)S(1)} %broadcast_compare_fusion), kind=kLoop, calls=%fused_computation.15 | loop fusion | flops 5898240 | bytes 3951380 | tf_op jit(solution)/shard_map/convert_element_type | solution.py:153
  102.5 7.3 %broadcast_multiply_fusion = f32[5,512,1024]{2,1,0:T(8,128)} fusion(bf16[5,512,256]{1,2,0:T(8,128)(2,1)S(1)} %fusion.4, bf16[5,512,1024]{2,1,0:T(8,128)(2,1)} %constant_dynamic-update-slice_fusion, s32[]{:T(128)S(6)} %select_n.293), kind=kOutput, calls=%fused_computation.9 | convolution fusion | flops 1344798720 | bytes 14417924 | tf_op jit(solution)/shard_map/prc,pcd->prd/dot_general | solution.py:156
  110.2 4.0 %broadcast_multiply_fusion.1 = f32[5,256,1024]{2,1,0:T(8,128)S(1)} fusion(bf16[5,512,256]{1,2,0:T(8,128)(2,1)S(1)} %fusion.4, bf16[5,512,1024]{2,1,0:T(8,128)(2,1)} %all-gather.2.cloned.1.call-done), kind=kOutput, calls=%fused_computation.21 | convolution fusion | flops 1343488000 | bytes 11796480 | tf_op jit(solution)/shard_map/prc,prd->pcd/dot_general | solution.py:160
  117.4 4.4 %collective-permute-start.21 = (f32[648,1024]{1,0:T(8,128)}, f32[648,1024]{1,0:T(8,128)}, u32[]{:S(2)}, u32[]{:S(2)}) collective-permute-start(f32[648,1024]{1,0:T(8,128)} %maximum_maximum_fusion), channel_id=1, source_target_pairs={{0,16},{16,0},{32,48},{48,32},{64,80},{80,64},{96,112},{112,96},{1... | collective-permute-start | bytes 7962632 | tf_op jit(solution)/shard_map/ppermute | solution.py:89
  121.8 4.9 %collective-permute-done.21 = f32[648,1024]{1,0:T(8,128)} collective-permute-done((f32[648,1024]{1,0:T(8,128)}, f32[648,1024]{1,0:T(8,128)}, u32[]{:S(2)}, u32[]{:S(2)}) %collective-permute-start.21) | collective-permute-done | bytes 2654240 | tf_op jit(solution)/shard_map/ppermute | solution.py:89
  132.2 16.5 %collective-permute-done.22 = f32[168,1024]{1,0:T(8,128)S(1)} collective-permute-done((f32[168,1024]{1,0:T(8,128)S(1)}, f32[168,1024]{1,0:T(8,128)S(1)}, u32[]{:S(2)}, u32[]{:S(2)}) %collective-permute-start.22) | collective-permute-done | bytes 688160 | tf_op jit(solution)/shard_map/ppermute | solution.py:102
  149.1 16.8 %collective-permute-done.23 = f32[168,1024]{1,0:T(8,128)S(1)} collective-permute-done((f32[168,1024]{1,0:T(8,128)S(1)}, f32[168,1024]{1,0:T(8,128)S(1)}, u32[]{:S(2)}, u32[]{:S(2)}) %collective-permute-start.23) | collective-permute-done | bytes 688160 | tf_op jit(solution)/shard_map/ppermute | solution.py:102
  167.0 2.8 %collective-permute-done.11 = f32[5]{0:T(128)S(1)} collective-permute-done((f32[5]{0:T(128)S(1)}, f32[5]{0:T(128)S(1)}, u32[]{:S(2)}, u32[]{:S(2)}) %collective-permute-start.11) | collective-permute-done | bytes 52 | tf_op jit(solution)/shard_map/ppermute | solution.py:50
  170.8 2.9 %collective-permute-done.12 = f32[5]{0:T(128)S(1)} collective-permute-done((f32[5]{0:T(128)S(1)}, f32[5]{0:T(128)S(1)}, u32[]{:S(2)}, u32[]{:S(2)}) %collective-permute-start.12) | collective-permute-done | bytes 52 | tf_op jit(solution)/shard_map/ppermute | solution.py:50
  173.7 2.7 %collective-permute-done.13 = f32[5]{0:T(128)S(1)} collective-permute-done((f32[5]{0:T(128)S(1)}, f32[5]{0:T(128)S(1)}, u32[]{:S(2)}, u32[]{:S(2)}) %collective-permute-start.13) | collective-permute-done | bytes 52 | tf_op jit(solution)/shard_map/ppermute | solution.py:50
  177.6 5.5 %collective-permute-done.24 = f32[168,1024]{1,0:T(8,128)S(1)} collective-permute-done((f32[168,1024]{1,0:T(8,128)}, f32[168,1024]{1,0:T(8,128)S(1)}, u32[]{:S(2)}, u32[]{:S(2)}) %collective-permute-start.24) | collective-permute-done | bytes 688160 | tf_op jit(solution)/shard_map/ppermute | solution.py:102
  184.8 15.2 %reduce-scatter.2.cloned.1.call-done = f32[5,32,1024]{2,1,0:T(8,128)} async-done(((f32[5,512,1024]{2,1,0:T(8,128)}), f32[5,32,1024]{2,1,0:T(8,128)}) %reduce-scatter.2.cloned.1.call-update) | async-done | bytes 655376 | tf_op jit(solution)/shard_map/reduce_scatter | solution.py:163
  200.1 2.4 %fusion.16 = (f32[5,32,1024]{2,1,0:T(8,128)}, f32[5,32,1024]{2,1,0:T(8,128)}) fusion(f32[5,32,1024]{2,1,0:T(8,128)S(1)} %bitcast.353, bf16[5,32,1024]{2,1,0:T(8,128)(2,1)S(1)} %copy-done.4, f32[5]{0:T(128)S(1)} %get-tuple-element.39, pred[5,32]{1,0:T(8,128)(4,1)S(1)} %broadcast_compare_fusion.2, f32[5,32,1024]{2,1,0:T(8,128)} %reduce-scatter.2.cloned.1.call-done, ...), kind=kLoop, calls=%fused_computation.38 | loop fusion | flops 1310720 | bytes 3276980 | tf_op jit(solution)/shard_map/jit(_where)/select_n | solution.py:176
  (139 shorter events, 55.2 us)
Async XLA Ops:
  7.2 62.7 %all-gather.2.cloned.1.call-start = ((), (), s32[]{:S(2)}) async-start(), calls=%async_computation.1 | async-start | bytes 5570560 | tf_op jit(solution)/shard_map/all_gather | solution.py:120
  7.9 192.2 %reduce-scatter.2.cloned.1.call-start = ((), (), s32[]{:S(2)}) async-start(), calls=%async_computation.2 | async-start | bytes 11141120 | tf_op jit(solution)/shard_map/reduce_scatter | solution.py:163
  8.0 6.9 %collective-permute-start = (bf16[5,32,1024]{2,1,0:T(8,128)(2,1)}, bf16[5,32,1024]{2,1,0:T(8,128)(2,1)S(1)}, u32[]{:S(2)}, u32[]{:S(2)}) collective-permute-start(bf16[5,32,1024]{2,1,0:T(8,128)(2,1)} %param.7), channel_id=1, source_target_pairs={{0,16},{16,32},{32,48},{48,64},{64,80},{80,96},{96,112},{112,0},{1... | collective-permute-start | bytes 983048 | tf_op jit(solution)/shard_map/ppermute | solution.py:71
  10.6 13.9 %collective-permute-start.4 = (bf16[5,32,1024]{2,1,0:T(8,128)(2,1)}, bf16[5,32,1024]{2,1,0:T(8,128)(2,1)S(1)}, u32[]{:S(2)}, u32[]{:S(2)}) collective-permute-start(bf16[5,32,1024]{2,1,0:T(8,128)(2,1)} %param.7), channel_id=1, source_target_pairs={{0,112},{16,0},{32,16},{48,32},{64,48},{80,64},{96,80},{112,96},{1... | collective-permute-start | bytes 983048 | tf_op jit(solution)/shard_map/ppermute | solution.py:74
  14.9 6.4 %collective-permute-start.1 = (bf16[5,32,1024]{2,1,0:T(8,128)(2,1)S(1)}, bf16[5,32,1024]{2,1,0:T(8,128)(2,1)S(1)}, u32[]{:S(2)}, u32[]{:S(2)}) collective-permute-start(bf16[5,32,1024]{2,1,0:T(8,128)(2,1)S(1)} %collective-permute-done), channel_id=1, source_target_pairs={{0,16},{16,32},{32,48},{48,64},{64,80},{80,96},{96,112},{112,0},{1... | collective-permute-start | bytes 983048 | tf_op jit(solution)/shard_map/ppermute | solution.py:71
  21.3 6.5 %collective-permute-start.2 = (bf16[5,32,1024]{2,1,0:T(8,128)(2,1)S(1)}, bf16[5,32,1024]{2,1,0:T(8,128)(2,1)S(1)}, u32[]{:S(2)}, u32[]{:S(2)}) collective-permute-start(bf16[5,32,1024]{2,1,0:T(8,128)(2,1)S(1)} %collective-permute-done.1), channel_id=1, source_target_pairs={{0,16},{16,32},{32,48},{48,64},{64,80},{80,96},{96,112},{112,0},{1... | collective-permute-start | bytes 983048 | tf_op jit(solution)/shard_map/ppermute | solution.py:71
  24.5 6.9 %collective-permute-start.5 = (bf16[5,32,1024]{2,1,0:T(8,128)(2,1)S(1)}, bf16[5,32,1024]{2,1,0:T(8,128)(2,1)S(1)}, u32[]{:S(2)}, u32[]{:S(2)}) collective-permute-start(bf16[5,32,1024]{2,1,0:T(8,128)(2,1)S(1)} %collective-permute-done.4), channel_id=1, source_target_pairs={{0,112},{16,0},{32,16},{48,32},{64,48},{80,64},{96,80},{112,96},{1... | collective-permute-start | bytes 983048 | tf_op jit(solution)/shard_map/ppermute | solution.py:74
  27.8 6.5 %collective-permute-start.3 = (bf16[5,32,1024]{2,1,0:T(8,128)(2,1)S(1)}, bf16[5,32,1024]{2,1,0:T(8,128)(2,1)S(1)}, u32[]{:S(2)}, u32[]{:S(2)}) collective-permute-start(bf16[5,32,1024]{2,1,0:T(8,128)(2,1)S(1)} %collective-permute-done.2), channel_id=1, source_target_pairs={{0,16},{16,32},{32,48},{48,64},{64,80},{80,96},{96,112},{112,0},{1... | collective-permute-start | bytes 983048 | tf_op jit(solution)/shard_map/ppermute | solution.py:71
  31.4 9.3 %collective-permute-start.6 = (bf16[5,32,1024]{2,1,0:T(8,128)(2,1)S(1)}, bf16[5,32,1024]{2,1,0:T(8,128)(2,1)S(1)}, u32[]{:S(2)}, u32[]{:S(2)}) collective-permute-start(bf16[5,32,1024]{2,1,0:T(8,128)(2,1)S(1)} %collective-permute-done.5), channel_id=1, source_target_pairs={{0,112},{16,0},{32,16},{48,32},{64,48},{80,64},{96,80},{112,96},{1... | collective-permute-start | bytes 983048 | tf_op jit(solution)/shard_map/ppermute | solution.py:74
  80.8 6.7 %collective-permute-start.10 = (f32[2,5,256]{2,1,0:T(8,128)S(1)}, f32[2,5,256]{2,1,0:T(8,128)S(1)}, u32[]{:S(2)}, u32[]{:S(2)}) collective-permute-start(f32[2,5,256]{2,1,0:T(8,128)S(1)} %get-tuple-element.34), channel_id=1, source_target_pairs={{0,96},{16,112},{32,0},{48,16},{64,32},{80,48},{96,64},{112,80},{1... | collective-permute-start | bytes 30728 | tf_op jit(solution)/shard_map/ppermute | solution.py:37
  83.3 4.8 %collective-permute-start.9 = (f32[2,5,256]{2,1,0:T(8,128)S(1)}, f32[2,5,256]{2,1,0:T(8,128)S(1)}, u32[]{:S(2)}, u32[]{:S(2)}) collective-permute-start(f32[2,5,256]{2,1,0:T(8,128)S(1)} %get-tuple-element.34), channel_id=1, source_target_pairs={{0,64},{16,80},{32,96},{48,112},{64,0},{80,16},{96,32},{112,48},{1... | collective-permute-start | bytes 30728 | tf_op jit(solution)/shard_map/ppermute | solution.py:37
  83.9 4.3 %collective-permute-start.8 = (f32[2,5,256]{2,1,0:T(8,128)S(1)}, f32[2,5,256]{2,1,0:T(8,128)S(1)}, u32[]{:S(2)}, u32[]{:S(2)}) collective-permute-start(f32[2,5,256]{2,1,0:T(8,128)S(1)} %get-tuple-element.34), channel_id=1, source_target_pairs={{0,32},{16,48},{32,64},{48,80},{64,96},{80,112},{96,0},{112,16},{1... | collective-permute-start | bytes 30728 | tf_op jit(solution)/shard_map/ppermute | solution.py:37
  84.5 4.3 %collective-permute-start.17 = (f32[3,5,512]{2,0,1:T(4,128)S(1)}, f32[3,5,512]{2,0,1:T(4,128)S(1)}, u32[]{:S(2)}, u32[]{:S(2)}) collective-permute-start(f32[3,5,512]{2,0,1:T(4,128)S(1)} %get-tuple-element.32), channel_id=1, source_target_pairs={{0,3},{1,0},{2,1},{3,2},{4,7},{5,4},{6,5},{7,6},{8,11},{9,8},{10,9... | collective-permute-start | bytes 92168 | tf_op jit(solution)/shard_map/ppermute | solution.py:37
  87.0 4.4 %collective-permute-start.16 = (f32[3,5,512]{2,0,1:T(4,128)S(1)}, f32[3,5,512]{2,0,1:T(4,128)S(1)}, u32[]{:S(2)}, u32[]{:S(2)}) collective-permute-start(f32[3,5,512]{2,0,1:T(4,128)S(1)} %get-tuple-element.32), channel_id=1, source_target_pairs={{0,2},{1,3},{2,0},{3,1},{4,6},{5,7},{6,4},{7,5},{8,10},{9,11},{10,... | collective-permute-start | bytes 92168 | tf_op jit(solution)/shard_map/ppermute | solution.py:37
  87.6 4.3 %collective-permute-start.15 = (f32[3,5,512]{2,0,1:T(4,128)S(1)}, f32[3,5,512]{2,0,1:T(4,128)S(1)}, u32[]{:S(2)}, u32[]{:S(2)}) collective-permute-start(f32[3,5,512]{2,0,1:T(4,128)S(1)} %get-tuple-element.32), channel_id=1, source_target_pairs={{0,1},{1,2},{2,3},{3,0},{4,5},{5,6},{6,7},{7,4},{8,9},{9,10},{10,1... | collective-permute-start | bytes 92168 | tf_op jit(solution)/shard_map/ppermute | solution.py:37
  92.8 2.9 %collective-permute-start.20 = (f32[3,5,512]{2,0,1:T(4,128)S(1)}, f32[3,5,512]{2,0,1:T(4,128)S(1)}, u32[]{:S(2)}, u32[]{:S(2)}) collective-permute-start(f32[3,5,512]{2,0,1:T(4,128)S(1)} %get-tuple-element.30), channel_id=1, source_target_pairs={{0,12},{1,13},{2,14},{3,15},{4,0},{5,1},{6,2},{7,3},{8,4},{9,5},{1... | collective-permute-start | bytes 92168 | tf_op jit(solution)/shard_map/ppermute | solution.py:37
  93.9 4.4 %collective-permute-start.19 = (f32[3,5,512]{2,0,1:T(4,128)S(1)}, f32[3,5,512]{2,0,1:T(4,128)S(1)}, u32[]{:S(2)}, u32[]{:S(2)}) collective-permute-start(f32[3,5,512]{2,0,1:T(4,128)S(1)} %get-tuple-element.30), channel_id=1, source_target_pairs={{0,8},{1,9},{2,10},{3,11},{4,12},{5,13},{6,14},{7,15},{8,0},{9,1},... | collective-permute-start | bytes 92168 | tf_op jit(solution)/shard_map/ppermute | solution.py:37
  94.6 4.1 %collective-permute-start.18 = (f32[3,5,512]{2,0,1:T(4,128)S(1)}, f32[3,5,512]{2,0,1:T(4,128)S(1)}, u32[]{:S(2)}, u32[]{:S(2)}) collective-permute-start(f32[3,5,512]{2,0,1:T(4,128)S(1)} %get-tuple-element.30), channel_id=1, source_target_pairs={{0,4},{1,5},{2,6},{3,7},{4,8},{5,9},{6,10},{7,11},{8,12},{9,13},{1... | collective-permute-start | bytes 92168 | tf_op jit(solution)/shard_map/ppermute | solution.py:37
  117.4 9.4 %collective-permute-start.21 = (f32[648,1024]{1,0:T(8,128)}, f32[648,1024]{1,0:T(8,128)}, u32[]{:S(2)}, u32[]{:S(2)}) collective-permute-start(f32[648,1024]{1,0:T(8,128)} %maximum_maximum_fusion), channel_id=1, source_target_pairs={{0,16},{16,0},{32,48},{48,32},{64,80},{80,64},{96,112},{112,96},{1... | collective-permute-start | bytes 7962632 | tf_op jit(solution)/shard_map/ppermute | solution.py:89
  130.7 18.0 %collective-permute-start.22 = (f32[168,1024]{1,0:T(8,128)S(1)}, f32[168,1024]{1,0:T(8,128)S(1)}, u32[]{:S(2)}, u32[]{:S(2)}) collective-permute-start(f32[168,1024]{1,0:T(8,128)S(1)} %pad_maximum_fusion.3), channel_id=1, source_target_pairs={{0,32},{16,48},{32,64},{48,80},{64,96},{80,112},{96,0},{112,16},{1... | collective-permute-start | bytes 2064392 | tf_op jit(solution)/shard_map/ppermute | solution.py:102
  148.8 17.1 %collective-permute-start.23 = (f32[168,1024]{1,0:T(8,128)S(1)}, f32[168,1024]{1,0:T(8,128)S(1)}, u32[]{:S(2)}, u32[]{:S(2)}) collective-permute-start(f32[168,1024]{1,0:T(8,128)S(1)} %fusion.12), channel_id=1, source_target_pairs={{0,32},{16,48},{32,64},{48,80},{64,96},{80,112},{96,0},{112,16},{1... | collective-permute-start | bytes 2064392 | tf_op jit(solution)/shard_map/ppermute | solution.py:102
  166.9 16.3 %collective-permute-start.24 = (f32[168,1024]{1,0:T(8,128)}, f32[168,1024]{1,0:T(8,128)S(1)}, u32[]{:S(2)}, u32[]{:S(2)}) collective-permute-start(f32[168,1024]{1,0:T(8,128)} %fusion.13), channel_id=1, source_target_pairs={{0,32},{16,48},{32,64},{48,80},{64,96},{80,112},{96,0},{112,16},{1... | collective-permute-start | bytes 2064392 | tf_op jit(solution)/shard_map/ppermute | solution.py:102
  169.8 3.9 %collective-permute-start.12 = (f32[5]{0:T(128)S(1)}, f32[5]{0:T(128)S(1)}, u32[]{:S(2)}, u32[]{:S(2)}) collective-permute-start(f32[5]{0:T(128)S(1)} %fusion.90), channel_id=1, source_target_pairs={{0,2},{1,3},{2,0},{3,1},{4,6},{5,7},{6,4},{7,5},{8,10},{9,11},{10,... | collective-permute-start | bytes 68 | tf_op jit(solution)/shard_map/ppermute | solution.py:50
  176.3 7.2 %collective-permute-start.14 = (f32[5]{0:T(128)S(1)}, f32[5]{0:T(128)S(1)}, u32[]{:S(2)}, u32[]{:S(2)}) collective-permute-start(f32[5]{0:T(128)S(1)} %fusion.88), channel_id=1, source_target_pairs={{0,8},{1,9},{2,10},{3,11},{4,12},{5,13},{6,14},{7,15},{8,0},{9,1},... | collective-permute-start | bytes 68 | tf_op jit(solution)/shard_map/ppermute | solution.py:50
  (9 other events, 173.8 us)
Sparse Core Ops, SparseCore 0:
  10.2 59.7 all-gather.1
  110.0 90.0 reduce-scatter.1
where the time goes:
time: 211 us; the launch traced here: 210 us
  waiting for transfers between devices  106 us (50%)
  starting transfers between devices  32.1 us (15%)
  local copies, waits for them, and re-layouts  20.9 us (10%)
  other arithmetic  18.4 us (9%)
  matrix products  16.5 us (8%)
  between operations  16.2 us (8%)
    ppermute x3, waiting for transfers between devices, two_stage_reduce_scatter(): running = lax.ppermute(running, axis, ring) + addend(chip - 1 - step)  38.8 us
    all_gather x1, waiting for transfers between devices, per_device(): row_set = lax.all_gather(anchor, 'pair', axis=1, tiled=True)  22.4 us
    reduce_scatter x1, waiting for transfers between devices, per_device(): lax.psum_scatter(grad_rows, 'pair', scatter_dimension=1, tiled=True)  15.2 us
    unnamed x28, local copies, waits for them, and re-layouts  14.9 us
    ppermute x10, starting transfers between devices, group_merge(): received.append(lax.ppermute(stats, axis, perm))  10.2 us
    ppermute x4, starting transfers between devices, ring_gather(): ahead = lax.ppermute(ahead, axis, forward)  9.95 us
    ppermute x4, waiting for transfers between devices, butterfly_sum(): other = lax.ppermute(values, axis, [(i, i ^ bit) for i in range(size)])  8.33 us
    ppermute x4, waiting for transfers between devices, ring_gather(): ahead = lax.ppermute(ahead, axis, forward)  7.61 us
  transfers between devices with their start and end apart: 27, of which 20 were waited for; matrix products, arithmetic and copies ran while one was open for 15% of the time, Pallas kernels for 0%

commit v1 on v0

--- a/solution.py
+++ b/solution.py
@@ -117,7 +117,9 @@
         jnp.sum(anchor.astype(jnp.float32) * partner.astype(jnp.float32), axis=2) * score_scale
     )
     own_positive = jnp.sum(jnp.where(own_valid, positive, 0.0), axis=1)
-    row_set = lax.all_gather(anchor, "pair", axis=1, tiled=True)
+    row_set = jnp.concatenate(
+        lax.all_to_all(jnp.stack([anchor] * lax.axis_size("pair")), "pair", 0, 0), axis=1
+    )
     col_set = jnp.concatenate(ring_gather(partner, "dp", dp_size), axis=1)
     col_set = jnp.roll(col_set, (dp_index - dp_size // 2) * shard_rows, axis=1)
     row_count = row_set.shape[1]

time: 211 us -> 244 us (1.16)
  starting transfers between devices: 32.1 us -> 48.9 us
  waiting for transfers between devices: 106 us -> 120 us
  local copies, waits for them, and re-layouts: 20.9 us -> 26.8 us
  other arithmetic: 18.4 us -> 13.8 us
    all_to_all x0 -> x1, waiting for transfers between devices: none -> 38.1 us  [per_device(): lax.all_to_all(jnp.stack([anchor] * lax.axis_size('pair')), 'pair', 0, 0)]
    all_gather x1 -> x0, waiting for transfers between devices: 22.4 us -> none  [per_device(): row_set = lax.all_gather(anchor, 'pair', axis=1, tiled=True)]
    all_to_all x0 -> x1, starting transfers between devices: none -> 8.79 us  [per_device(): lax.all_to_all(jnp.stack([anchor] * lax.axis_size('pair')), 'pair', 0, 0)]
    ppermute x10, starting transfers between devices: 10.2 us -> 15.7 us  [group_merge(): received.append(lax.ppermute(stats, axis, perm))]
    ppermute x3, starting transfers between devices: 3.18 us -> 8.22 us  [ring_gather(): behind = lax.ppermute(behind, axis, backward)]
    another operation x0 -> x1, local copies, waits for them, and re-layouts: none -> 3.99 us  [per_device(): jnp.stack([anchor] * lax.axis_size('pair'))]
    ppermute x10, waiting for transfers between devices: 7.35 us -> 3.45 us  [group_merge(): received.append(lax.ppermute(stats, axis, perm))]
    reshape x0 -> x1, local copies, waits for them, and re-layouts: none -> 3.12 us  [per_device(): jnp.concatenate(lax.all_to_all(jnp.stack([anchor] * lax.axis_size('pair')...]
  transfers between devices with their start and end apart: 27 -> 27, of which waited for: 20 -> 19; matrix products, arithmetic and copies ran while one was open for 15% -> 10% of each run, Pallas kernels for 0% -> 0%
where the time goes in v1:
time: 244 us; the launch traced here: 243 us
  waiting for transfers between devices  120 us (49%)
  starting transfers between devices  48.9 us (20%)
  local copies, waits for them, and re-layouts  26.8 us (11%)
  matrix products  16.9 us (7%)
  between operations  16.3 us (7%)
  other arithmetic  13.8 us (6%)
    ppermute x3, waiting for transfers between devices, two_stage_reduce_scatter(): running = lax.ppermute(running, axis, ring) + addend(chip - 1 - step)  38.8 us
    all_to_all x1, waiting for transfers between devices, per_device(): lax.all_to_all(jnp.stack([anchor] * lax.axis_size('pair')), 'pair', 0, 0)  38.1 us
    reduce_scatter x1, waiting for transfers between devices, per_device(): lax.psum_scatter(grad_rows, 'pair', scatter_dimension=1, tiled=True)  16.8 us
    ppermute x10, starting transfers between devices, group_merge(): received.append(lax.ppermute(stats, axis, perm))  15.7 us
    unnamed x32, local copies, waits for them, and re-layouts  13.7 us
    ppermute x4, waiting for transfers between devices, ring_gather(): ahead = lax.ppermute(ahead, axis, forward)  9.33 us
    all_to_all x1, starting transfers between devices, per_device(): lax.all_to_all(jnp.stack([anchor] * lax.axis_size('pair')), 'pair', 0, 0)  8.79 us
    ppermute x4, waiting for transfers between devices, butterfly_sum(): other = lax.ppermute(values, axis, [(i, i ^ bit) for i in range(size)])  8.62 us
  transfers between devices with their start and end apart: 27, of which 19 were waited for; matrix products, arithmetic and copies ran while one was open for 10% of the time, Pallas kernels for 0%

profile of v1, /device:TPU:1, one launch (start us, length us, event | category | flops | bytes accessed | tf_op | source)
XLA Modules:
  0.0 243.2 jit_solution(3293816412200358991)
XLA Ops:
  7.2 4.0 %stack.92 = bf16[16,5,32,1024]{3,2,1,0:T(8,128)(2,1)} broadcast(bf16[5,32,1024]{2,1,0:T(8,128)(2,1)} %param.6), dimensions={1,2,3} | broadcast | bytes 5570560 | tf_op jit(solution)/shard_map/stack | solution.py:121
  11.2 8.8 %all-to-all-start = ((bf16[16,5,32,1024]{3,2,1,0:T(8,128)(2,1)}), bf16[16,5,32,1024]{3,2,1,0:T(8,128)(2,1)}, u32[]{:S(2)}, u32[]{:S(2)}) async-start(bf16[16,5,32,1024]{3,2,1,0:T(8,128)(2,1)} %stack.92), calls=%async_computation | async-start | bytes 10485760 | tf_op jit(solution)/shard_map/all_to_all | solution.py:121
  22.8 3.3 %collective-permute-done = bf16[5,32,1024]{2,1,0:T(8,128)(2,1)S(1)} collective-permute-done((bf16[5,32,1024]{2,1,0:T(8,128)(2,1)S(1)}, bf16[5,32,1024]{2,1,0:T(8,128)(2,1)S(1)}, u32[]{:S(2)}, u32[]{:S(2)}) %collective-permute-start) | collective-permute-done | bytes 327712 | tf_op jit(solution)/shard_map/ppermute | solution.py:71
  28.7 3.9 %collective-permute-done.1 = bf16[5,32,1024]{2,1,0:T(8,128)(2,1)S(1)} collective-permute-done((bf16[5,32,1024]{2,1,0:T(8,128)(2,1)S(1)}, bf16[5,32,1024]{2,1,0:T(8,128)(2,1)S(1)}, u32[]{:S(2)}, u32[]{:S(2)}) %collective-permute-start.1) | collective-permute-done | bytes 327712 | tf_op jit(solution)/shard_map/ppermute | solution.py:71
  35.2 3.2 %collective-permute-start.5 = (bf16[5,32,1024]{2,1,0:T(8,128)(2,1)S(1)}, bf16[5,32,1024]{2,1,0:T(8,128)(2,1)S(1)}, u32[]{:S(2)}, u32[]{:S(2)}) collective-permute-start(bf16[5,32,1024]{2,1,0:T(8,128)(2,1)S(1)} %collective-permute-done.4), channel_id=1, source_target_pairs={{0,112},{16,0},{32,16},{48,32},{64,48},{80,64},{96,80},{112,96},{1... | collective-permute-start | bytes 983048 | tf_op jit(solution)/shard_map/ppermute | solution.py:74
  42.1 4.0 %collective-permute-start.6 = (bf16[5,32,1024]{2,1,0:T(8,128)(2,1)S(1)}, bf16[5,32,1024]{2,1,0:T(8,128)(2,1)S(1)}, u32[]{:S(2)}, u32[]{:S(2)}) collective-permute-start(bf16[5,32,1024]{2,1,0:T(8,128)(2,1)S(1)} %collective-permute-done.5), channel_id=1, source_target_pairs={{0,112},{16,0},{32,16},{48,32},{64,48},{80,64},{96,80},{112,96},{1... | collective-permute-start | bytes 983048 | tf_op jit(solution)/shard_map/ppermute | solution.py:74
  59.2 38.1 %all-to-all-done = bf16[16,5,32,1024]{3,2,1,0:T(8,128)(2,1)} async-done(((bf16[16,5,32,1024]{3,2,1,0:T(8,128)(2,1)}), bf16[16,5,32,1024]{3,2,1,0:T(8,128)(2,1)}, u32[]{:S(2)}, u32[]{:S(2)}) %all-to-all-start) | async-done | bytes 5242912 | tf_op jit(solution)/shard_map/all_to_all | solution.py:121
  97.3 3.1 %copy.54 = bf16[5,16,32,1024]{3,2,1,0:T(8,128)(2,1)S(1)} copy(bf16[5,16,32,1024]{3,2,0,1:T(8,128)(2,1)} %bitcast) | data formatting | bytes 10485760 | tf_op jit(solution)/shard_map/reshape | solution.py:120
  100.4 5.5 %fusion.11 = (f32[5,256]{1,0:T(8,128)S(1)}, f32[5,512]{1,0:T(8,128)S(1)}, f32[5,256,512]{2,1,0:T(8,128)S(1)}) fusion(pred[5,256]{1,0:T(8,128)(4,1)S(1)} %broadcast_compare_fusion.1, pred[5,512]{1,0:T(8,128)(4,1)S(1)} %broadcast_compare_fusion, bf16[5,512,1024]{2,1,0:T(8,128)(2,1)S(1)} %bitcast.349, ...), kind=kOutput, calls=%fused_computation.30 | convolution fusion | flops 1345450240 | bytes 10504964 | tf_op jit(solution)/shard_map/prd,pcd->prc/dot_general | solution.py:134
  112.9 2.8 %collective-permute-start.9 = (f32[2,5,256]{2,1,0:T(8,128)S(1)}, f32[2,5,256]{2,1,0:T(8,128)S(1)}, u32[]{:S(2)}, u32[]{:S(2)}) collective-permute-start(f32[2,5,256]{2,1,0:T(8,128)S(1)} %get-tuple-element.34), channel_id=1, source_target_pairs={{0,64},{16,80},{32,96},{48,112},{64,0},{80,16},{96,32},{112,48},{1... | collective-permute-start | bytes 30728 | tf_op jit(solution)/shard_map/ppermute | solution.py:37
  124.4 2.8 %collective-permute-start.19 = (f32[3,5,512]{2,0,1:T(4,128)S(1)}, f32[3,5,512]{2,0,1:T(4,128)S(1)}, u32[]{:S(2)}, u32[]{:S(2)}) collective-permute-start(f32[3,5,512]{2,0,1:T(4,128)S(1)} %get-tuple-element.30), channel_id=1, source_target_pairs={{0,8},{1,9},{2,10},{3,11},{4,12},{5,13},{6,14},{7,15},{8,0},{9,1},... | collective-permute-start | bytes 92168 | tf_op jit(solution)/shard_map/ppermute | solution.py:37
  127.2 2.7 %collective-permute-start.20 = (f32[3,5,512]{2,0,1:T(4,128)S(1)}, f32[3,5,512]{2,0,1:T(4,128)S(1)}, u32[]{:S(2)}, u32[]{:S(2)}) collective-permute-start(f32[3,5,512]{2,0,1:T(4,128)S(1)} %get-tuple-element.30), channel_id=1, source_target_pairs={{0,12},{1,13},{2,14},{3,15},{4,0},{5,1},{6,2},{7,3},{8,4},{9,5},{1... | collective-permute-start | bytes 92168 | tf_op jit(solution)/shard_map/ppermute | solution.py:37
  132.3 2.7 %fusion.4 = bf16[5,512,256]{1,2,0:T(8,128)(2,1)S(1)} fusion(f32[5,256,512]{2,1,0:T(8,128)} %copy-done.3, f32[5,256]{1,0:T(8,128)S(1)} %get-tuple-element.9, f32[5,512]{1,0:T(8,128)S(1)} %get-tuple-element.13, f32[5]{0:T(128)S(1)} %get-tuple-element.40, pred[5,256]{1,0:T(8,128)(4,1)S(1)} %broadcast_compare_fusion.1, pred[5,512]{1,0:T(8,128)(4,1)S(1)} %broadcast_compare_fusion), kind=kLoop, calls=%fused_computation.15 | loop fusion | flops 5898240 | bytes 3951380 | tf_op jit(solution)/shard_map/convert_element_type | solution.py:155
  135.1 7.3 %broadcast_multiply_fusion = f32[5,512,1024]{2,1,0:T(8,128)} fusion(bf16[5,512,256]{1,2,0:T(8,128)(2,1)S(1)} %fusion.4, bf16[5,512,1024]{2,1,0:T(8,128)(2,1)} %constant_dynamic-update-slice_fusion, s32[]{:T(128)S(6)} %select_n.293), kind=kOutput, calls=%fused_computation.9 | convolution fusion | flops 1344798720 | bytes 14417924 | tf_op jit(solution)/shard_map/prc,pcd->prd/dot_general | solution.py:158
  142.8 4.0 %broadcast_multiply_fusion.1 = f32[5,256,1024]{2,1,0:T(8,128)S(1)} fusion(bf16[5,512,256]{1,2,0:T(8,128)(2,1)S(1)} %fusion.4, bf16[5,512,1024]{2,1,0:T(8,128)(2,1)} %bitcast.350), kind=kOutput, calls=%fused_computation.21 | convolution fusion | flops 1343488000 | bytes 11796480 | tf_op jit(solution)/shard_map/prc,prd->pcd/dot_general | solution.py:162
  149.9 4.1 %collective-permute-start.21 = (f32[648,1024]{1,0:T(8,128)}, f32[648,1024]{1,0:T(8,128)}, u32[]{:S(2)}, u32[]{:S(2)}) collective-permute-start(f32[648,1024]{1,0:T(8,128)} %maximum_maximum_fusion), channel_id=1, source_target_pairs={{0,16},{16,0},{32,48},{48,32},{64,80},{80,64},{96,112},{112,96},{1... | collective-permute-start | bytes 7962632 | tf_op jit(solution)/shard_map/ppermute | solution.py:89
  154.0 4.9 %collective-permute-done.21 = f32[648,1024]{1,0:T(8,128)} collective-permute-done((f32[648,1024]{1,0:T(8,128)}, f32[648,1024]{1,0:T(8,128)}, u32[]{:S(2)}, u32[]{:S(2)}) %collective-permute-start.21) | collective-permute-done | bytes 2654240 | tf_op jit(solution)/shard_map/ppermute | solution.py:89
  163.0 18.0 %collective-permute-done.22 = f32[168,1024]{1,0:T(8,128)S(1)} collective-permute-done((f32[168,1024]{1,0:T(8,128)S(1)}, f32[168,1024]{1,0:T(8,128)S(1)}, u32[]{:S(2)}, u32[]{:S(2)}) %collective-permute-start.22) | collective-permute-done | bytes 688160 | tf_op jit(solution)/shard_map/ppermute | solution.py:102
  181.1 17.0 %collective-permute-done.23 = f32[168,1024]{1,0:T(8,128)S(1)} collective-permute-done((f32[168,1024]{1,0:T(8,128)S(1)}, f32[168,1024]{1,0:T(8,128)S(1)}, u32[]{:S(2)}, u32[]{:S(2)}) %collective-permute-start.23) | collective-permute-done | bytes 688160 | tf_op jit(solution)/shard_map/ppermute | solution.py:102
  198.4 2.8 %collective-permute-done.11 = f32[5]{0:T(128)S(1)} collective-permute-done((f32[5]{0:T(128)S(1)}, f32[5]{0:T(128)S(1)}, u32[]{:S(2)}, u32[]{:S(2)}) %collective-permute-start.11) | collective-permute-done | bytes 52 | tf_op jit(solution)/shard_map/ppermute | solution.py:50
  202.0 3.1 %collective-permute-done.12 = f32[5]{0:T(128)S(1)} collective-permute-done((f32[5]{0:T(128)S(1)}, f32[5]{0:T(128)S(1)}, u32[]{:S(2)}, u32[]{:S(2)}) %collective-permute-start.12) | collective-permute-done | bytes 52 | tf_op jit(solution)/shard_map/ppermute | solution.py:50
  205.1 2.8 %collective-permute-done.13 = f32[5]{0:T(128)S(1)} collective-permute-done((f32[5]{0:T(128)S(1)}, f32[5]{0:T(128)S(1)}, u32[]{:S(2)}, u32[]{:S(2)}) %collective-permute-start.13) | collective-permute-done | bytes 52 | tf_op jit(solution)/shard_map/ppermute | solution.py:50
  210.6 3.8 %collective-permute-done.24 = f32[168,1024]{1,0:T(8,128)S(1)} collective-permute-done((f32[168,1024]{1,0:T(8,128)S(1)}, f32[168,1024]{1,0:T(8,128)S(1)}, u32[]{:S(2)}, u32[]{:S(2)}) %collective-permute-start.24) | collective-permute-done | bytes 688160 | tf_op jit(solution)/shard_map/ppermute | solution.py:102
  216.0 16.8 %reduce-scatter.2.cloned.1.call-done = f32[5,32,1024]{2,1,0:T(8,128)} async-done(((f32[5,512,1024]{2,1,0:T(8,128)}), f32[5,32,1024]{2,1,0:T(8,128)}) %reduce-scatter.2.cloned.1.call-update) | async-done | bytes 655376 | tf_op jit(solution)/shard_map/reduce_scatter | solution.py:165
  (144 shorter events, 57.2 us)
Async XLA Ops:
  11.2 86.1 %all-to-all-start = ((bf16[16,5,32,1024]{3,2,1,0:T(8,128)(2,1)}), bf16[16,5,32,1024]{3,2,1,0:T(8,128)(2,1)}, u32[]{:S(2)}, u32[]{:S(2)}) async-start(bf16[16,5,32,1024]{3,2,1,0:T(8,128)(2,1)} %stack.92), calls=%async_computation | async-start | bytes 10485760 | tf_op jit(solution)/shard_map/all_to_all | solution.py:121
  20.0 212.9 %reduce-scatter.2.cloned.1.call-start = ((), (), s32[]{:S(2)}) async-start(), calls=%async_computation.2 | async-start | bytes 11141120 | tf_op jit(solution)/shard_map/reduce_scatter | solution.py:165
  20.0 15.2 %collective-permute-start.4 = (bf16[5,32,1024]{2,1,0:T(8,128)(2,1)S(1)}, bf16[5,32,1024]{2,1,0:T(8,128)(2,1)S(1)}, u32[]{:S(2)}, u32[]{:S(2)}) collective-permute-start(bf16[5,32,1024]{2,1,0:T(8,128)(2,1)S(1)} %copy-done.4), channel_id=1, source_target_pairs={{0,112},{16,0},{32,16},{48,32},{64,48},{80,64},{96,80},{112,96},{1... | collective-permute-start | bytes 983048 | tf_op jit(solution)/shard_map/ppermute | solution.py:74
  21.0 5.1 %collective-permute-start = (bf16[5,32,1024]{2,1,0:T(8,128)(2,1)S(1)}, bf16[5,32,1024]{2,1,0:T(8,128)(2,1)S(1)}, u32[]{:S(2)}, u32[]{:S(2)}) collective-permute-start(bf16[5,32,1024]{2,1,0:T(8,128)(2,1)S(1)} %copy-done.4), channel_id=1, source_target_pairs={{0,16},{16,32},{32,48},{48,64},{64,80},{80,96},{96,112},{112,0},{1... | collective-permute-start | bytes 983048 | tf_op jit(solution)/shard_map/ppermute | solution.py:71
  26.1 6.5 %collective-permute-start.1 = (bf16[5,32,1024]{2,1,0:T(8,128)(2,1)S(1)}, bf16[5,32,1024]{2,1,0:T(8,128)(2,1)S(1)}, u32[]{:S(2)}, u32[]{:S(2)}) collective-permute-start(bf16[5,32,1024]{2,1,0:T(8,128)(2,1)S(1)} %collective-permute-done), channel_id=1, source_target_pairs={{0,16},{16,32},{32,48},{48,64},{64,80},{80,96},{96,112},{112,0},{1... | collective-permute-start | bytes 983048 | tf_op jit(solution)/shard_map/ppermute | solution.py:71
  32.6 6.8 %collective-permute-start.2 = (bf16[5,32,1024]{2,1,0:T(8,128)(2,1)S(1)}, bf16[5,32,1024]{2,1,0:T(8,128)(2,1)S(1)}, u32[]{:S(2)}, u32[]{:S(2)}) collective-permute-start(bf16[5,32,1024]{2,1,0:T(8,128)(2,1)S(1)} %collective-permute-done.1), channel_id=1, source_target_pairs={{0,16},{16,32},{32,48},{48,64},{64,80},{80,96},{96,112},{112,0},{1... | collective-permute-start | bytes 983048 | tf_op jit(solution)/shard_map/ppermute | solution.py:71
  35.2 6.9 %collective-permute-start.5 = (bf16[5,32,1024]{2,1,0:T(8,128)(2,1)S(1)}, bf16[5,32,1024]{2,1,0:T(8,128)(2,1)S(1)}, u32[]{:S(2)}, u32[]{:S(2)}) collective-permute-start(bf16[5,32,1024]{2,1,0:T(8,128)(2,1)S(1)} %collective-permute-done.4), channel_id=1, source_target_pairs={{0,112},{16,0},{32,16},{48,32},{64,48},{80,64},{96,80},{112,96},{1... | collective-permute-start | bytes 983048 | tf_op jit(solution)/shard_map/ppermute | solution.py:74
  39.4 7.7 %collective-permute-start.3 = (bf16[5,32,1024]{2,1,0:T(8,128)(2,1)S(1)}, bf16[5,32,1024]{2,1,0:T(8,128)(2,1)S(1)}, u32[]{:S(2)}, u32[]{:S(2)}) collective-permute-start(bf16[5,32,1024]{2,1,0:T(8,128)(2,1)S(1)} %collective-permute-done.2), channel_id=1, source_target_pairs={{0,16},{16,32},{32,48},{48,64},{64,80},{80,96},{96,112},{112,0},{1... | collective-permute-start | bytes 983048 | tf_op jit(solution)/shard_map/ppermute | solution.py:71
  42.1 10.3 %collective-permute-start.6 = (bf16[5,32,1024]{2,1,0:T(8,128)(2,1)S(1)}, bf16[5,32,1024]{2,1,0:T(8,128)(2,1)S(1)}, u32[]{:S(2)}, u32[]{:S(2)}) collective-permute-start(bf16[5,32,1024]{2,1,0:T(8,128)(2,1)S(1)} %collective-permute-done.5), channel_id=1, source_target_pairs={{0,112},{16,0},{32,16},{48,32},{64,48},{80,64},{96,80},{112,96},{1... | collective-permute-start | bytes 983048 | tf_op jit(solution)/shard_map/ppermute | solution.py:74
  112.9 7.4 %collective-permute-start.9 = (f32[2,5,256]{2,1,0:T(8,128)S(1)}, f32[2,5,256]{2,1,0:T(8,128)S(1)}, u32[]{:S(2)}, u32[]{:S(2)}) collective-permute-start(f32[2,5,256]{2,1,0:T(8,128)S(1)} %get-tuple-element.34), channel_id=1, source_target_pairs={{0,64},{16,80},{32,96},{48,112},{64,0},{80,16},{96,32},{112,48},{1... | collective-permute-start | bytes 30728 | tf_op jit(solution)/shard_map/ppermute | solution.py:37
  115.7 5.6 %collective-permute-start.8 = (f32[2,5,256]{2,1,0:T(8,128)S(1)}, f32[2,5,256]{2,1,0:T(8,128)S(1)}, u32[]{:S(2)}, u32[]{:S(2)}) collective-permute-start(f32[2,5,256]{2,1,0:T(8,128)S(1)} %get-tuple-element.34), channel_id=1, source_target_pairs={{0,32},{16,48},{32,64},{48,80},{64,96},{80,112},{96,0},{112,16},{1... | collective-permute-start | bytes 30728 | tf_op jit(solution)/shard_map/ppermute | solution.py:37
  116.0 5.3 %collective-permute-start.10 = (f32[2,5,256]{2,1,0:T(8,128)S(1)}, f32[2,5,256]{2,1,0:T(8,128)S(1)}, u32[]{:S(2)}, u32[]{:S(2)}) collective-permute-start(f32[2,5,256]{2,1,0:T(8,128)S(1)} %get-tuple-element.34), channel_id=1, source_target_pairs={{0,96},{16,112},{32,0},{48,16},{64,32},{80,48},{96,64},{112,80},{1... | collective-permute-start | bytes 30728 | tf_op jit(solution)/shard_map/ppermute | solution.py:37
  118.4 4.5 %collective-permute-start.16 = (f32[3,5,512]{2,0,1:T(4,128)S(1)}, f32[3,5,512]{2,0,1:T(4,128)S(1)}, u32[]{:S(2)}, u32[]{:S(2)}) collective-permute-start(f32[3,5,512]{2,0,1:T(4,128)S(1)} %get-tuple-element.32), channel_id=1, source_target_pairs={{0,2},{1,3},{2,0},{3,1},{4,6},{5,7},{6,4},{7,5},{8,10},{9,11},{10,... | collective-permute-start | bytes 92168 | tf_op jit(solution)/shard_map/ppermute | solution.py:37
  118.5 4.6 %collective-permute-start.15 = (f32[3,5,512]{2,0,1:T(4,128)S(1)}, f32[3,5,512]{2,0,1:T(4,128)S(1)}, u32[]{:S(2)}, u32[]{:S(2)}) collective-permute-start(f32[3,5,512]{2,0,1:T(4,128)S(1)} %get-tuple-element.32), channel_id=1, source_target_pairs={{0,1},{1,2},{2,3},{3,0},{4,5},{5,6},{6,7},{7,4},{8,9},{9,10},{10,1... | collective-permute-start | bytes 92168 | tf_op jit(solution)/shard_map/ppermute | solution.py:37
  120.2 3.1 %collective-permute-start.17 = (f32[3,5,512]{2,0,1:T(4,128)S(1)}, f32[3,5,512]{2,0,1:T(4,128)S(1)}, u32[]{:S(2)}, u32[]{:S(2)}) collective-permute-start(f32[3,5,512]{2,0,1:T(4,128)S(1)} %get-tuple-element.32), channel_id=1, source_target_pairs={{0,3},{1,0},{2,1},{3,2},{4,7},{5,4},{6,5},{7,6},{8,11},{9,8},{10,9... | collective-permute-start | bytes 92168 | tf_op jit(solution)/shard_map/ppermute | solution.py:37
  124.4 5.7 %collective-permute-start.19 = (f32[3,5,512]{2,0,1:T(4,128)S(1)}, f32[3,5,512]{2,0,1:T(4,128)S(1)}, u32[]{:S(2)}, u32[]{:S(2)}) collective-permute-start(f32[3,5,512]{2,0,1:T(4,128)S(1)} %get-tuple-element.30), channel_id=1, source_target_pairs={{0,8},{1,9},{2,10},{3,11},{4,12},{5,13},{6,14},{7,15},{8,0},{9,1},... | collective-permute-start | bytes 92168 | tf_op jit(solution)/shard_map/ppermute | solution.py:37
  127.2 4.1 %collective-permute-start.18 = (f32[3,5,512]{2,0,1:T(4,128)S(1)}, f32[3,5,512]{2,0,1:T(4,128)S(1)}, u32[]{:S(2)}, u32[]{:S(2)}) collective-permute-start(f32[3,5,512]{2,0,1:T(4,128)S(1)} %get-tuple-element.30), channel_id=1, source_target_pairs={{0,4},{1,5},{2,6},{3,7},{4,8},{5,9},{6,10},{7,11},{8,12},{9,13},{1... | collective-permute-start | bytes 92168 | tf_op jit(solution)/shard_map/ppermute | solution.py:37
  127.2 4.1 %collective-permute-start.20 = (f32[3,5,512]{2,0,1:T(4,128)S(1)}, f32[3,5,512]{2,0,1:T(4,128)S(1)}, u32[]{:S(2)}, u32[]{:S(2)}) collective-permute-start(f32[3,5,512]{2,0,1:T(4,128)S(1)} %get-tuple-element.30), channel_id=1, source_target_pairs={{0,12},{1,13},{2,14},{3,15},{4,0},{5,1},{6,2},{7,3},{8,4},{9,5},{1... | collective-permute-start | bytes 92168 | tf_op jit(solution)/shard_map/ppermute | solution.py:37
  149.9 9.1 %collective-permute-start.21 = (f32[648,1024]{1,0:T(8,128)}, f32[648,1024]{1,0:T(8,128)}, u32[]{:S(2)}, u32[]{:S(2)}) collective-permute-start(f32[648,1024]{1,0:T(8,128)} %maximum_maximum_fusion), channel_id=1, source_target_pairs={{0,16},{16,0},{32,48},{48,32},{64,80},{80,64},{96,112},{112,96},{1... | collective-permute-start | bytes 7962632 | tf_op jit(solution)/shard_map/ppermute | solution.py:89
  162.9 18.0 %collective-permute-start.22 = (f32[168,1024]{1,0:T(8,128)S(1)}, f32[168,1024]{1,0:T(8,128)S(1)}, u32[]{:S(2)}, u32[]{:S(2)}) collective-permute-start(f32[168,1024]{1,0:T(8,128)S(1)} %pad_maximum_fusion.3), channel_id=1, source_target_pairs={{0,32},{16,48},{32,64},{48,80},{64,96},{80,112},{96,0},{112,16},{1... | collective-permute-start | bytes 2064392 | tf_op jit(solution)/shard_map/ppermute | solution.py:102
  181.0 17.1 %collective-permute-start.23 = (f32[168,1024]{1,0:T(8,128)S(1)}, f32[168,1024]{1,0:T(8,128)S(1)}, u32[]{:S(2)}, u32[]{:S(2)}) collective-permute-start(f32[168,1024]{1,0:T(8,128)S(1)} %fusion.12), channel_id=1, source_target_pairs={{0,32},{16,48},{32,64},{48,80},{64,96},{80,112},{96,0},{112,16},{1... | collective-permute-start | bytes 2064392 | tf_op jit(solution)/shard_map/ppermute | solution.py:102
  198.2 16.2 %collective-permute-start.24 = (f32[168,1024]{1,0:T(8,128)S(1)}, f32[168,1024]{1,0:T(8,128)S(1)}, u32[]{:S(2)}, u32[]{:S(2)}) collective-permute-start(f32[168,1024]{1,0:T(8,128)S(1)} %fusion.13), channel_id=1, source_target_pairs={{0,32},{16,48},{32,64},{48,80},{64,96},{80,112},{96,0},{112,16},{1... | collective-permute-start | bytes 2064392 | tf_op jit(solution)/shard_map/ppermute | solution.py:102
  201.2 3.9 %collective-permute-start.12 = (f32[5]{0:T(128)S(1)}, f32[5]{0:T(128)S(1)}, u32[]{:S(2)}, u32[]{:S(2)}) collective-permute-start(f32[5]{0:T(128)S(1)} %fusion.90), channel_id=1, source_target_pairs={{0,2},{1,3},{2,0},{3,1},{4,6},{5,7},{6,4},{7,5},{8,10},{9,11},{10,... | collective-permute-start | bytes 68 | tf_op jit(solution)/shard_map/ppermute | solution.py:50
  207.9 6.9 %collective-permute-start.14 = (f32[5]{0:T(128)S(1)}, f32[5]{0:T(128)S(1)}, u32[]{:S(2)}, u32[]{:S(2)}) collective-permute-start(f32[5]{0:T(128)S(1)} %fusion.88), channel_id=1, source_target_pairs={{0,8},{1,9},{2,10},{3,11},{4,12},{5,13},{6,14},{7,15},{8,0},{9,1},... | collective-permute-start | bytes 68 | tf_op jit(solution)/shard_map/ppermute | solution.py:50
  (11 other events, 68.6 us)
Sparse Core Ops, SparseCore 0:
  142.5 90.2 reduce-scatter.1
